TPU v7x, 128 devices: a whole 4x4x4 slice. The times are simulated.
128 devices in a mesh: row: 4 (over x), col: 32 (over z, y, core).
Axes of the slice: x: 4, y: 4, z: 4, core: 2. Of those that a mesh axis runs over, the one named last changes fastest.
Arguments:
- child_factors: bfloat16 [2, 2048, 8192], P(None, 'col', 'row'), may hold values from -0.0625 to 0.0625
- child_tiles: int32 [2, 16], replicated, may hold values from 0 to 63, as said below
- root_diag: float32 [8192], P('col'), may hold values from 0.5 to 4
Outputs:
- front_out: float32 [8192, 8192], P('row', 'col')
Inputs may be any that keep to these rules, and one draw needn't show every extreme that they name: `child_tiles`: each row lists 2048 / 128 distinct root tiles in increasing order; the first child's list holds tile 0 and the second child's holds the last tile. For every r below 4, exactly 2048 / (128 * 4) tiles t of each row have ((t * 128) // 256) % 4 == r.
All inputs are finite; a program needn't handle non-finite values.
Results may differ from a plain program's by a relative error of at most 0.0003.
Values may be sent and summed in bfloat16 or wider, within the bound.
No kernel may reach another device: no remote copies, remote signals or barrier semaphores. Data moves between devices by JAX's collectives and lax.ppermute only.
A program may use at most 128 MiB of HBM per device.

v0:
```python
import jax
import jax.numpy as jnp
from jax import lax
from jax.sharding import PartitionSpec as P

TILE = 128
NPAN = 1


def broadcast(block, axis, source):
    block = jnp.where(lax.axis_index(axis) == source, block, jnp.zeros_like(block))
    return lax.psum(block, axis)


def pivot_factor(source, local_block, owner_row, block_size, identity, usable):
    diag_rows = source[local_block * block_size : (local_block + 1) * block_size]
    pivots = broadcast(diag_rows, "row", owner_row)
    return jnp.linalg.cholesky(jnp.where(usable, pivots, identity))


def solve_panel(source, factor, row_block, panel_step, blocks_here):
    solved = lax.linalg.triangular_solve(
        factor, source, left_side=False, lower=True, transpose_a=True
    )
    repeated = jnp.tile(jnp.tril(factor), (blocks_here, 1))
    later = (row_block > panel_step)[:, None]
    current = (row_block == panel_step)[:, None]
    return jnp.where(later, solved, jnp.where(current, repeated, 0.0))


def shards(child_factors, child_tiles, root_diag):
    highest = lax.Precision.HIGHEST
    row_count = lax.axis_size("row")
    col_count = lax.axis_size("col")
    block_size = root_diag.shape[0]
    order_total = block_size * col_count
    loc_rows = order_total // row_count
    blocks_here = loc_rows // block_size
    row_index = lax.axis_index("row")
    col_index = lax.axis_index("col")
    gathered = lax.all_gather(child_factors, "col", axis=1, tiled=True)
    tile_total = gathered.shape[1] // TILE
    tiles_per_col = block_size // TILE
    wanted = col_index * tiles_per_col + jnp.arange(tiles_per_col, dtype=jnp.int32)
    selector = (child_tiles[:, :, None] == wanted[None, None, :]).astype(jnp.bfloat16)
    tiled_rows = gathered.reshape(2, tile_total, TILE, gathered.shape[2])
    own_cols = jnp.einsum(
        "cui,cutk->citk", selector, tiled_rows, preferred_element_type=jnp.float32
    )
    own_cols = own_cols.astype(jnp.bfloat16).reshape(2, block_size, gathered.shape[2])
    partial_gram = jnp.einsum(
        "cnk,cmk->cnm", gathered, own_cols, preferred_element_type=jnp.float32
    )
    gram_tiles = partial_gram.reshape(2, tile_total, TILE, block_size)
    stored_tile = jnp.arange(lax.axis_size("row") * loc_rows // TILE, dtype=jnp.int32)
    stored_row = stored_tile * TILE
    owning = stored_row // loc_rows
    within = stored_row % loc_rows
    global_row = (owning + within // block_size * row_count) * block_size + within % block_size
    global_tile = global_row // TILE
    matches = (child_tiles[:, :, None] == global_tile[None, None, :]).astype(jnp.float32)
    placed = jnp.einsum("cus,cutm->stm", matches, gram_tiles, precision=highest)
    assembled = lax.psum_scatter(
        placed.reshape(lax.axis_size("row") * loc_rows, block_size),
        "row",
        scatter_dimension=0,
        tiled=True,
    )
    local_rows = jnp.arange(loc_rows, dtype=jnp.int32)
    row_block = row_index + local_rows // block_size * row_count
    glob_rows = row_block * block_size + local_rows % block_size
    glob_cols = col_index * block_size + jnp.arange(block_size, dtype=jnp.int32)
    front_now = assembled + jnp.where(
        glob_rows[:, None] == glob_cols[None, :], root_diag[None, :], 0.0
    )
    identity = jnp.eye(block_size, dtype=jnp.float32)
    owner_row = 0 % row_count
    local_block = 0 // row_count
    factor = pivot_factor(front_now, local_block, owner_row, block_size, identity, col_index == 0)
    own_panel = solve_panel(front_now, factor, row_block, 0, blocks_here)
    panel_block = broadcast(own_panel, "col", 0)
    own_block = lax.dynamic_slice_in_dim(
        panel_block, col_index // row_count * block_size, block_size, 0
    )
    across = broadcast(own_block.astype(jnp.bfloat16), "row", col_index % row_count).astype(
        own_block.dtype
    )
    update = jnp.dot(panel_block, across.T, precision=highest)
    front_now = jnp.where(col_index == 0, panel_block, front_now - update)
    upper_part = (row_block[:, None] < NPAN) & (col_index >= NPAN)
    return jnp.where(upper_part, 0.0, front_now)


def solution(mesh):
    placed = (P(None, "col", "row"), P(), P("col"))
    return jax.shard_map(
        shards, mesh=mesh, in_specs=placed, out_specs=P("row", "col"), check_vma=False
    )
```

profile of v0, /device:TPU:0, one launch (start us, length us, event | category | flops | bytes accessed | tf_op | source)
XLA Modules:
  0.0 501.5 jit_solution(1409809897628505502)
XLA Ops:
  6.5 0.0 all-gather.2.cloned.1.call-start
  6.5 0.7 all-gather.2.cloned.1.call-update
  7.3 0.0 reduce-scatter.2.cloned.1.call-start
  7.4 77.5 %all-gather.2.cloned.1.call-done = bf16[2,2048,2048]{2,1,0:T(8,128)(2,1)} async-done(((bf16[2,64,2048]{2,1,0:T(8,128)(2,1)}), bf16[2,2048,2048]{2,1,0:T(8,128)(2,1)}) %all-gather.2.cloned.1.call-update) | async-done | bytes 16777232 | tf_op jit(solution)/shard_map/all_gather | solution.py:41
  84.8 24.6 %fusion.2 = bf16[2,2,128,2048]{3,1,2,0:T(2,128)(2,1)S(1)} fusion(bf16[2,16,128,2048]{3,2,1,0:T(8,128)(2,1)} %bitcast.68, s32[2,16]{1,0:T(2,128)} %param.4, s32[2]{0:T(128)S(1)} %iota_add_fusion.1), kind=kOutput, calls=%fused_computation.5 | convolution fusion | flops 34603072 | bytes 18874504 | tf_op jit(solution)/shard_map/cui,cutk->citk/dot_general | solution.py:47
  109.5 2.2 copy.14
  111.7 13.0 %fusion.43 = f32[2,256,2048]{2,1,0:T(8,128)} fusion(bf16[2,256,2048]{2,1,0:T(8,128)(2,1)} %bitcast.73, bf16[2,2048,2048]{2,1,0:T(8,128)(2,1)} %all-gather.2.cloned.1.call-done), kind=kOutput, calls=%fused_computation.88 | convolution fusion | flops 4294967296 | bytes 23068672 | tf_op jit(solution)/shard_map/cnk,cmk->cnm/dot_general | solution.py:51
  124.7 0.0 copy-start.1
  124.7 3.1 copy.31
  127.8 0.0 copy-done.1
  127.9 3.6 fusion.21
  131.5 11.1 %copy.39 = f32[32,8,64,128]{3,1,2,0:T(8,128)} copy(f32[32,8,64,128]{3,2,1,0:T(8,128)S(1)} %bitcast.67) | data formatting | bytes 16777216
  142.6 0.0 copy-start.2
  142.6 0.0 reduce-scatter.2.cloned.1.call-update
  142.6 0.0 all-reduce.5.cloned.1.call-start
  142.7 80.0 %reduce-scatter.2.cloned.1.call-done = f32[2048,256]{0,1:T(8,128)} async-done(((f32[8192,256]{0,1:T(8,128)}), f32[2048,256]{0,1:T(8,128)}) %reduce-scatter.2.cloned.1.call-update) | async-done | bytes 2097168 | tf_op jit(solution)/shard_map/reduce_scatter | solution.py:63
  222.7 0.0 copy-done.2
  222.7 1.9 select_add_fusion
  224.5 0.7 slice_select_fusion
  225.3 0.0 all-reduce.5.cloned.1.call-update
  225.3 0.0 all-reduce.7.cloned.1.call-start
  225.4 41.6 %all-reduce.5.cloned.1.call-done = f32[256,256]{0,1:T(8,128)} async-done(((f32[256,256]{0,1:T(8,128)}), f32[256,256]{0,1:T(8,128)}) %all-reduce.5.cloned.1.call-update) | async-done | bytes 262160 | tf_op jit(solution)/shard_map/psum | solution.py:12
  267.0 1.0 convert_select_fusion
  267.9 0.1 copy.17
  268.1 1.0 fusion.10
  269.1 11.7 %cholesky.49 = f32[128,128]{1,0:T(8,128)S(1)} custom-call(f32[128,128]{1,0:T(8,128)S(1)} %cholesky.115), custom_call_target="Cholesky" | custom-call | tf_op jit(solution)/shard_map/jit(cholesky)/cholesky | solution.py:18
  280.8 9.8 %custom-call.14 = f32[1,128,128]{1,2,0:T(8,128)S(1)} custom-call(f32[1,128,128]{2,1,0:T(8,128)S(1)} %get-tuple-element.32), custom_call_target="InvertDiagBlocksLowerTriangular" | custom-call | tf_op jit(solution)/shard_map/jit(cholesky)/cholesky | solution.py:18
  290.7 0.2 fusion.14
  290.9 0.3 convolution_subtract_fusion.2
  291.1 11.7 %cholesky.103 = f32[128,128]{1,0:T(8,128)S(1)} custom-call(f32[128,128]{1,0:T(8,128)S(1)} %convolution_subtract_fusion.2), custom_call_target="Cholesky" | custom-call | tf_op jit(solution)/shard_map/jit(cholesky)/cholesky | solution.py:18
  302.9 0.1 copy.20
  303.0 0.1 copy.19
  303.1 0.1 copy.18
  303.2 0.7 compare_reduce_fusion
  305.4 0.1 tile.4
  305.5 2.2 copy.33
  307.7 0.1 triangular_solve.61
  307.8 4.5 while.1
  308.0 0.7 fusion.54
  308.7 1.3 dynamic-slice.7
  310.0 0.1 copy.41
  310.2 0.7 fusion.54
  310.8 1.3 dynamic-slice.7
  312.2 0.1 copy.41
  312.3 19.7 %custom-call.15 = f32[2,128,128]{1,2,0:T(8,128)S(1)} custom-call(f32[2,128,128]{2,1,0:T(8,128)S(1)} %get-tuple-element.12), custom_call_target="InvertDiagBlocksLowerTriangular" | custom-call | tf_op jit(solution)/shard_map/triangular_solve | solution.py:22
  332.0 1.1 fusion.8
  333.1 0.0 copy-start
  333.1 1.1 convolution_subtract_fusion.1
  334.2 1.1 fusion.12
  335.3 0.0 copy-done
  335.3 1.7 fusion.7
  337.0 0.0 all-reduce.7.cloned.1.call-update
  337.0 0.0 all-reduce.9.cloned.1.call-start
  337.1 106.4 %all-reduce.7.cloned.1.call-done = f32[2048,256]{0,1:T(8,128)} async-done(((f32[2048,256]{0,1:T(8,128)}), f32[2048,256]{0,1:T(8,128)}) %all-reduce.7.cloned.1.call-update) | async-done | bytes 2097168 | tf_op jit(solution)/shard_map/psum | solution.py:12
  443.5 1.6 fusion.11
  445.1 0.0 all-reduce.9.cloned.1.call-update
  445.1 41.5 %all-reduce.9.cloned.1.call-done = bf16[256,256]{0,1:T(8,128)(2,1)} async-done(((bf16[256,256]{0,1:T(8,128)(2,1)}), bf16[256,256]{0,1:T(8,128)(2,1)}) %all-reduce.9.cloned.1.call-update) | async-done | bytes 131088 | tf_op jit(solution)/shard_map/psum | solution.py:12
  486.7 5.0 fusion.6
  491.6 2.9 copy.23
  (19 shorter events, 0.3 us)
Async XLA Ops:
  6.5 78.3 %all-gather.2.cloned.1.call-start = ((), (), s32[]{:S(2)}) async-start(), calls=%async_computation.1 | async-start | bytes 17301504 | tf_op jit(solution)/shard_map/all_gather | solution.py:41
  7.3 215.4 %reduce-scatter.2.cloned.1.call-start = ((), (), s32[]{:S(2)}) async-start(), calls=%async_computation.2 | async-start | bytes 10485760 | tf_op jit(solution)/shard_map/reduce_scatter | solution.py:63
  124.7 3.1 copy-start.1
  142.6 80.1 %copy-start.2 = (f32[256]{0:T(256)S(1)}, f32[256]{0:T(256)}, u32[]{:S(2)}) copy-start(f32[256]{0:T(256)} %param.5) | copy-start | bytes 3076
  142.6 124.4 %all-reduce.5.cloned.1.call-start = ((), (), s32[]{:S(2)}) async-start(), calls=%async_computation.3 | async-start | bytes 524288 | tf_op jit(solution)/shard_map/psum | solution.py:12
  225.3 218.2 %all-reduce.7.cloned.1.call-start = ((), (), s32[]{:S(2)}) async-start(), calls=%async_computation.4 | async-start | bytes 4194304 | tf_op jit(solution)/shard_map/psum | solution.py:12
  333.1 2.2 copy-start
  337.0 149.7 %all-reduce.9.cloned.1.call-start = ((), (), s32[]{:S(2)}) async-start(), calls=%async_computation.5 | async-start | bytes 262144 | tf_op jit(solution)/shard_map/psum | solution.py:12
Sparse Core Ops, SparseCore 0:
  9.6 75.1 all-gather.1
  142.7 79.8 reduce-scatter.1
  225.4 41.5 all-reduce.4
  337.1 106.3 all-reduce.6
  445.6 40.9 all-reduce.8
where the time goes:
time: 510 us; the launch traced here: 501 us
  waiting for transfers between devices  348 us (68%)
  other arithmetic  61.7 us (12%)
  matrix products  50 us (10%)
  local copies, waits for them, and re-layouts  26.4 us (5%)
  between operations  15.2 us (3%)
    psum x3, waiting for transfers between devices, broadcast(): return lax.psum(block, axis)  190 us
    reduce_scatter x1, waiting for transfers between devices, shards(): lax.psum_scatter(placed.reshape(lax.axis_size('row') * loc_rows, block_si...  80 us
    all_gather x1, waiting for transfers between devices, shards(): gathered = lax.all_gather(child_factors, 'col', axis=1, tiled=True)  77.5 us
    another operation x6, other arithmetic, pivot_factor(): return jnp.linalg.cholesky(jnp.where(usable, pivots, identity))  34 us
    dot_general x1, matrix products, shards(): jnp.einsum('cui,cutk->citk', selector, tiled_rows, preferred_element_type...  24.6 us
    another operation x3, other arithmetic, solve_panel(): lax.linalg.triangular_solve(factor, source, left_side=False, lower=True,...  19.7 us
    unnamed x9, local copies, waits for them, and re-layouts  16.4 us
    dot_general x1, matrix products, shards(): jnp.einsum('cnk,cmk->cnm', gathered, own_cols, preferred_element_type=jnp...  13 us
  transfers between devices with their start and end apart: 5, of which 5 were waited for; matrix products, arithmetic and copies ran while one was open for 0% of the time, Pallas kernels for 0%

commit v1 on v0

--- a/solution.py
+++ b/solution.py
@@ -7,9 +7,15 @@
 NPAN = 1
 
 
+def add_all(x, name):
+    parts = lax.all_gather(x, name, axis=0, tiled=False)
+    acc = parts.sum(axis=0)
+    return acc
+
+
 def broadcast(block, axis, source):
     block = jnp.where(lax.axis_index(axis) == source, block, jnp.zeros_like(block))
-    return lax.psum(block, axis)
+    return add_all(block, axis)
 
 
 def pivot_factor(source, local_block, owner_row, block_size, identity, usable):

time: 510 us -> 589 us (1.15)
  waiting for transfers between devices: 348 us -> 383 us
  other arithmetic: 61.7 us -> 82.2 us
  blocking collectives: 0 us -> 13.1 us
  local copies, waits for them, and re-layouts: 26.4 us -> 33.9 us
    all_gather x0 -> x2, waiting for transfers between devices: none -> 225 us  [add_all(): parts = lax.all_gather(x, name, axis=0, tiled=False)]
    psum x3 -> x0, waiting for transfers between devices: 190 us -> none  [broadcast(): return lax.psum(block, axis)]
    unnamed x1 -> x2, other arithmetic: 0.01 us -> 22.2 us
    all_gather x0 -> x1, blocking collectives: none -> 13.1 us  [add_all(): parts = lax.all_gather(x, name, axis=0, tiled=False)]
    unnamed x9 -> x8, local copies, waits for them, and re-layouts: 16.4 us -> 5.14 us
    dot_general x0 -> x1, local copies, waits for them, and re-layouts: none -> 8.08 us  [shards(): placed = jnp.einsum('cus,cutm->stm', matches, gram_tiles, precision=highest)]
  transfers between devices with their start and end apart: 5 -> 4, of which waited for: 5 -> 4; matrix products, arithmetic and copies ran while one was open for 0% -> 0% of each run, Pallas kernels for 0% -> 0%
where the time goes in v1:
time: 589 us; the launch traced here: 580 us
  waiting for transfers between devices  383 us (65%)
  other arithmetic  82.2 us (14%)
  matrix products  52.2 us (9%)
  local copies, waits for them, and re-layouts  33.9 us (6%)
  between operations  14.9 us (3%)
  blocking collectives  13.1 us (2%)
    all_gather x2, waiting for transfers between devices, add_all(): parts = lax.all_gather(x, name, axis=0, tiled=False)  225 us
    reduce_scatter x1, waiting for transfers between devices, shards(): lax.psum_scatter(placed.reshape(lax.axis_size('row') * loc_rows, block_si...  80 us
    all_gather x1, waiting for transfers between devices, shards(): gathered = lax.all_gather(child_factors, 'col', axis=1, tiled=True)  77.5 us
    another operation x6, other arithmetic, pivot_factor(): return jnp.linalg.cholesky(jnp.where(usable, pivots, identity))  34 us
    dot_general x1, matrix products, shards(): jnp.einsum('cui,cutk->citk', selector, tiled_rows, preferred_element_type...  24.5 us
    unnamed x2, other arithmetic  22.2 us
    another operation x3, other arithmetic, solve_panel(): lax.linalg.triangular_solve(factor, source, left_side=False, lower=True,...  19.7 us
    all_gather x1, blocking collectives, add_all(): parts = lax.all_gather(x, name, axis=0, tiled=False)  13.1 us
  transfers between devices with their start and end apart: 4, of which 4 were waited for; matrix products, arithmetic and copies ran while one was open for 0% of the time, Pallas kernels for 0%

profile of v1, /device:TPU:0, one launch (start us, length us, event | category | flops | bytes accessed | tf_op | source)
XLA Modules:
  0.0 580.1 jit_solution(9197356112321010637)
XLA Ops:
  6.5 0.0 all-gather.6.cloned.1.call-start
  6.5 0.7 all-gather.6.cloned.1.call-update
  7.3 0.0 reduce-scatter.2.cloned.1.call-start
  7.4 77.5 %all-gather.6.cloned.1.call-done = bf16[2,2048,2048]{2,1,0:T(8,128)(2,1)} async-done(((bf16[2,64,2048]{2,1,0:T(8,128)(2,1)}), bf16[2,2048,2048]{2,1,0:T(8,128)(2,1)}) %all-gather.6.cloned.1.call-update) | async-done | bytes 16777232 | tf_op jit(solution)/shard_map/all_gather | solution.py:47
  84.8 24.5 %fusion.2 = bf16[2,2,128,2048]{3,1,2,0:T(2,128)(2,1)S(1)} fusion(bf16[2,16,128,2048]{3,2,1,0:T(8,128)(2,1)} %bitcast.68, s32[2,16]{1,0:T(2,128)} %param.4, s32[2]{0:T(128)S(1)} %iota_add_fusion.1), kind=kOutput, calls=%fused_computation.5 | convolution fusion | flops 34603072 | bytes 18874504 | tf_op jit(solution)/shard_map/cui,cutk->citk/dot_general | solution.py:53
  109.3 2.2 copy.26
  111.5 13.1 %fusion.41 = f32[2,256,2048]{2,1,0:T(8,128)} fusion(bf16[2,256,2048]{2,1,0:T(8,128)(2,1)} %bitcast.72, bf16[2,2048,2048]{2,1,0:T(8,128)(2,1)} %all-gather.6.cloned.1.call-done), kind=kOutput, calls=%fused_computation.88 | convolution fusion | flops 4294967296 | bytes 23068672 | tf_op jit(solution)/shard_map/cnk,cmk->cnm/dot_general | solution.py:57
  124.6 5.0 copy.38
  129.6 0.0 copy-start.1
  129.6 5.6 copy.27
  135.3 0.0 copy-done.1
  135.3 5.5 convolution_bitcast_fusion
  140.8 8.1 %copy.28 = f32[64,128,256]{2,1,0:T(8,128)} copy(f32[64,128,256]{2,0,1:T(8,128)S(1)} %convolution_bitcast_fusion) | data formatting | bytes 16777216 | tf_op jit(solution)/shard_map/cus,cutm->stm/dot_general | solution.py:68
  148.9 0.0 copy-start.2
  148.9 0.0 reduce-scatter.2.cloned.1.call-update
  148.9 0.0 all-gather.10.cloned.1.call-start
  149.0 80.0 %reduce-scatter.2.cloned.1.call-done = f32[2048,256]{1,0:T(8,128)} async-done(((f32[8192,256]{1,0:T(8,128)}), f32[2048,256]{1,0:T(8,128)}) %reduce-scatter.2.cloned.1.call-update) | async-done | bytes 2097168 | tf_op jit(solution)/shard_map/reduce_scatter | solution.py:69
  229.0 0.0 copy-done.2
  229.0 1.8 select_add_fusion
  230.8 0.7 slice_select_fusion
  231.5 0.0 all-gather.10.cloned.1.call-update
  231.5 0.4 all-gather.8.cloned.1.call-start
  232.0 23.5 %all-gather.10.cloned.1.call-done = f32[1024,256]{1,0:T(8,128)} async-done(((f32[256,256]{1,0:T(8,128)}), f32[1024,256]{1,0:T(8,128)}) %all-gather.10.cloned.1.call-update) | async-done | bytes 1048592 | tf_op jit(solution)/shard_map/all_gather | solution.py:11
  255.5 1.3 reduce_sum.32
  256.8 0.1 copy.29
  256.9 0.1 fusion.11
  257.0 11.7 %cholesky.49 = f32[128,128]{1,0:T(8,128)S(1)} custom-call(f32[128,128]{1,0:T(8,128)S(1)} %cholesky.115), custom_call_target="Cholesky" | custom-call | tf_op jit(solution)/shard_map/jit(cholesky)/cholesky | solution.py:24
  268.8 9.8 %custom-call.14 = f32[1,128,128]{1,2,0:T(8,128)S(1)} custom-call(f32[1,128,128]{2,1,0:T(8,128)S(1)} %get-tuple-element.26), custom_call_target="InvertDiagBlocksLowerTriangular" | custom-call | tf_op jit(solution)/shard_map/jit(cholesky)/cholesky | solution.py:24
  278.6 0.2 constant_dynamic-update-slice_fusion.1
  278.8 0.3 convolution_subtract_fusion.2
  279.1 11.7 %cholesky.103 = f32[128,128]{1,0:T(8,128)S(1)} custom-call(f32[128,128]{1,0:T(8,128)S(1)} %convolution_subtract_fusion.2), custom_call_target="Cholesky" | custom-call | tf_op jit(solution)/shard_map/jit(cholesky)/cholesky | solution.py:24
  290.8 0.7 compare_reduce_fusion
  292.9 0.1 copy.30
  293.1 1.5 tile.4
  294.5 2.9 tile.10
  297.4 0.1 triangular_solve.68
  297.5 3.9 while.1
  297.5 0.6 fusion.52
  298.1 1.3 bitcast_dynamic-update-slice_fusion.2
  299.5 0.6 fusion.52
  300.0 1.3 bitcast_dynamic-update-slice_fusion.2
  301.4 19.7 %custom-call.15 = f32[2,128,128]{1,2,0:T(8,128)S(1)} custom-call(f32[2,128,128]{2,1,0:T(8,128)S(1)} %get-tuple-element.12), custom_call_target="InvertDiagBlocksLowerTriangular" | custom-call | tf_op jit(solution)/shard_map/triangular_solve | solution.py:28
  321.1 1.1 fusion.8
  322.2 0.0 copy-start
  322.2 1.8 convolution_subtract_fusion.1
  324.0 1.1 convolution_bitcast_fusion.1
  325.1 0.0 copy-done
  325.1 1.7 fusion.7
  326.8 2.9 copy.31
  329.7 0.0 all-gather.8.cloned.1.call-update
  329.8 201.6 %all-gather.8.cloned.1.call-done = f32[32,2048,256]{2,1,0:T(8,128)} async-done(((f32[1,2048,256]{2,1,0:T(8,128)}), f32[32,2048,256]{2,1,0:T(8,128)}) %all-gather.8.cloned.1.call-update) | async-done | bytes 67108880 | tf_op jit(solution)/shard_map/all_gather | solution.py:11
  531.4 22.2 %reduce_sum.34 = f32[2048,256]{1,0:T(8,128)} reduce(f32[32,2048,256]{2,1,0:T(8,128)} %all-gather.8.cloned.1.call-done, f32[]{:T(128)} %constant.197.clone.1), dimensions={0}, to_apply=%region_6.7 | reduce | flops 16252928 | bytes 69206016
  553.5 1.0 constant_dynamic-slice_fusion.1
  554.5 0.1 copy.37
  554.6 13.1 %all-gather.1 = bf16[1024,256]{0,1:T(8,128)(2,1)S(1)} all-gather(bf16[256,256]{0,1:T(8,128)(2,1)S(1)} %convert_select_fusion), channel_id=3, replica_groups=mesh['row'=4,'col'=32] {'row'}, dimensions={0}, use_global_device_ids=true | all-gather | bytes 655360 | tf_op jit(solution)/shard_map/all_gather | solution.py:11
  567.7 0.4 reshape.261
  568.1 0.7 reduce_sum.35
  568.8 4.7 fusion.6
  (16 shorter events, 0.2 us)
Async XLA Ops:
  6.5 78.3 %all-gather.6.cloned.1.call-start = ((), (), s32[]{:S(2)}) async-start(), calls=%async_computation.1 | async-start | bytes 17301504 | tf_op jit(solution)/shard_map/all_gather | solution.py:47
  7.3 221.7 %reduce-scatter.2.cloned.1.call-start = ((), (), s32[]{:S(2)}) async-start(), calls=%async_computation.2 | async-start | bytes 10485760 | tf_op jit(solution)/shard_map/reduce_scatter | solution.py:69
  129.6 5.6 copy-start.1
  148.9 80.1 %copy-start.2 = (f32[256]{0:T(256)S(1)}, f32[256]{0:T(256)}, u32[]{:S(2)}) copy-start(f32[256]{0:T(256)} %param.5) | copy-start | bytes 3076
  148.9 106.5 %all-gather.10.cloned.1.call-start = ((), (), s32[]{:S(2)}) async-start(), calls=%async_computation.4 | async-start | bytes 1310720 | tf_op jit(solution)/shard_map/all_gather | solution.py:11
  231.5 299.9 %all-gather.8.cloned.1.call-start = ((), (), s32[]{:S(2)}) async-start(), calls=%async_computation.3 | async-start | bytes 69206016 | tf_op jit(solution)/shard_map/all_gather | solution.py:11
  322.2 2.9 copy-start
Sparse Core Ops, SparseCore 0:
  9.6 75.1 all-gather.5
  149.0 79.8 reduce-scatter.1
  231.6 23.7 all-gather.9
  329.9 201.4 all-gather.7
